TPU v7x, 128 devices: a whole 4x4x4 slice. The times are simulated.
128 devices in a mesh: seq: 16 (over z, x), heads: 8 (over y, core).
Axes of the slice: x: 4, y: 4, z: 4, core: 2. Of those that a mesh axis runs over, the one named last changes fastest.
Arguments:
- audio: bfloat16 [4096, 1280], P('seq'), may hold values from -6 to 6
- ln_gain: float32 [1280], replicated, may hold values from 0.25 to 1.75
- ln_shift: float32 [1280], replicated, may hold values from -3 to 3
- enc_wq: bfloat16 [1280, 1024], P(None, 'heads'), may hold values from -0.15625 to 0.15625
- enc_bq: float32 [1024], P('heads'), may hold values from -3 to 3
- enc_wk: bfloat16 [1280, 1024], P(None, 'heads'), may hold values from -4 to 4
- enc_wv: bfloat16 [1280, 1024], P(None, 'heads'), may hold values from -0.15625 to 0.15625
- enc_bv: float32 [1024], P('heads'), may hold values from -3 to 3
- enc_wo: bfloat16 [1024, 1280], P('heads'), may hold values from -0.1875 to 0.1875
- enc_bo: float32 [1280], replicated, may hold values from -3 to 3
- windows: int32 [16], P('heads'), may hold values from 1 to 128, as said below
- dec_wkv: bfloat16 [1280, 8, 256], replicated, may hold values from -4 to 4
- dec_bv: float32 [8, 128], replicated, may hold values from -3 to 3
- text: bfloat16 [8192, 8192], P('seq'), may hold values from -6 to 6
- norm_gain: float32 [8192], replicated, may hold values from 0.25 to 1.75
- dec_wq: bfloat16 [8192, 4096], P('seq', 'heads'), may hold values from -0.0625 to 0.0625
- dec_bq: float32 [4096], P('heads'), may hold values from -3 to 3
- dec_wo: bfloat16 [4096, 8192], P('heads', 'seq'), may hold values from -0.125 to 0.125
- span_start: int32 [8192], P('seq'), may hold values from 0 to 3840, as said below
- span_len: int32 [8192], P('seq'), may hold values from 1 to 256, as said below
Outputs:
- enc_out: bfloat16 [4096, 1280], P(('seq', 'heads'))
- dec_out: bfloat16 [8192, 8192], P('seq', 'heads')
Inputs may be any that keep to these rules, and one draw needn't show every extreme that they name: `windows`: every head's window is 1 to 128; some head has exactly 128 and some head exactly 1. `span_start`: row r's band begins between r * 256 // 512 - 255 and r * 256 // 512, and never before frame 0 or after 4096 - 256; row 0 begins at 0 and the last row at 3840; the last row of every aligned block of 512 rows but the final one begins exactly at r * 256 // 512. `span_len`: row 0 has 256 valid frames and row 1 has one; the last row of every aligned block of 512 rows has 256, unless it is row 1.
All inputs are finite; a program needn't handle non-finite values.
Results may differ from a plain program's by a relative error of at most 0.025.
Values may be sent and summed in bfloat16 or wider, within the bound.
No kernel may reach another device: no remote copies, remote signals or barrier semaphores. Data moves between devices by JAX's collectives and lax.ppermute only.
A program may use at most 128 MiB of HBM per device.

v0:
```python
import jax
import jax.numpy as jnp
from jax import lax
from jax.sharding import PartitionSpec as P

EWIN = 128
BAND = 256


def with_halo(block, sides, width):
    for axis, dim in sides:
        count = lax.axis_size(axis)
        forward = [(i, i + 1) for i in range(count - 1)]
        backward = [(target, source) for source, target in forward]
        low = lax.ppermute(
            lax.slice_in_dim(block, block.shape[dim] - width, None, axis=dim), axis, forward
        )
        high = lax.ppermute(lax.slice_in_dim(block, 0, width, axis=dim), axis, backward)
        block = jnp.concatenate([low, block, high], axis=dim)
    return block


def heads_gather(block, axis):
    count = lax.axis_size(axis)
    index = lax.axis_index(axis)
    gathered = block[None]
    bit = 1
    while bit < count:
        other = lax.ppermute(gathered, axis, [(i, i ^ bit) for i in range(count)])
        upper = index & bit != 0
        gathered = jnp.where(
            upper,
            jnp.concatenate([other, gathered], axis=0),
            jnp.concatenate([gathered, other], axis=0),
        )
        bit *= 2
    return gathered


def heads_ring_gather(block, axis):
    count = lax.axis_size(axis)
    ring = count // 2
    index = lax.axis_index(axis)
    chip = index // 2
    core = index % 2
    swap = [(i, i ^ 1) for i in range(count)]
    sibling = lax.ppermute(block, axis, swap)
    own = jnp.where(core == 0, jnp.stack([block, sibling]), jnp.stack([sibling, block]))
    step = []
    for i in range(count):
        direction = 1 if i % 2 == 0 else -1
        step.append((i, (i // 2 + direction) % ring * 2 + i % 2))
    near = lax.ppermute(own, axis, step)
    far = lax.ppermute(near, axis, step)
    other = lax.ppermute(near, axis, swap)
    sign = 1 - 2 * core
    owners = [chip, (chip - sign) % ring, (chip + 2) % ring, (chip + sign) % ring]
    return ([own, near, far, other], owners)


def layer_norm(values, gain, shift):
    values = values.astype(jnp.float32)
    centre = values - jnp.mean(values, axis=-1, keepdims=True)
    spread = jnp.mean(centre * centre, axis=-1, keepdims=True)
    return centre * lax.rsqrt(spread + 1e-05) * gain + shift


def rms_norm(values, gain):
    values = values.astype(jnp.float32)
    return values * lax.rsqrt(jnp.mean(values * values, axis=-1, keepdims=True) + 1e-06) * gain


def masked_softmax(scores, valid):
    highest = jnp.max(jnp.where(valid, scores, -jnp.inf), axis=-1, keepdims=True)
    raised = jnp.where(valid, jnp.exp(scores - highest), jnp.zeros_like(scores))
    return (raised / jnp.sum(raised, axis=-1, keepdims=True)).astype(jnp.bfloat16)


def shards(
    audio,
    ln_gain,
    ln_shift,
    enc_wq,
    enc_bq,
    enc_wk,
    enc_wv,
    enc_bv,
    enc_wo,
    enc_bo,
    windows,
    dec_wkv,
    dec_bv,
    text,
    norm_gain,
    dec_wq,
    dec_bq,
    dec_wo,
    span_start,
    span_len,
):
    seq_count = lax.axis_size("seq")
    head_count = lax.axis_size("heads")
    seq_index = lax.axis_index("seq")
    head_index = lax.axis_index("heads")
    frames_dev = audio.shape[0]
    enc_width = audio.shape[1]
    heads_dev = windows.shape[0]
    head_size = enc_wq.shape[1] // heads_dev
    all_frames = frames_dev * seq_count
    hidden = layer_norm(audio, ln_gain, ln_shift).astype(jnp.bfloat16)
    enc_query = (jnp.dot(hidden, enc_wq, preferred_element_type=jnp.float32) + enc_bq).astype(
        jnp.bfloat16
    )
    enc_keys = jnp.dot(hidden, enc_wk, preferred_element_type=jnp.float32).astype(jnp.bfloat16)
    enc_values = (jnp.dot(hidden, enc_wv, preferred_element_type=jnp.float32) + enc_bv).astype(
        jnp.bfloat16
    )
    enc_pairs = jnp.stack([enc_keys, enc_values], axis=1)
    widened = with_halo(enc_pairs, (("seq", 0),), EWIN)
    extent = frames_dev + 2 * EWIN
    key_block = widened[:, 0, :].reshape(extent, heads_dev, head_size)
    value_block = widened[:, 1, :].reshape(extent, heads_dev, head_size)
    query_block = enc_query.reshape(frames_dev, heads_dev, head_size)
    scores = jnp.einsum(
        "qhd,khd->hqk", query_block, key_block, preferred_element_type=jnp.float32
    ) * head_size ** (-0.5)
    row_frames = seq_index * frames_dev + jnp.arange(frames_dev, dtype=jnp.int32)
    col_frames = seq_index * frames_dev - EWIN + jnp.arange(extent, dtype=jnp.int32)
    distance = jnp.abs(row_frames[:, None] - col_frames[None, :])
    inside = (col_frames >= 0) & (col_frames < all_frames)
    valid = (distance[None, :, :] <= windows[:, None, None]) & inside[None, None, :]
    enc_weights = masked_softmax(scores, valid)
    enc_context = jnp.einsum(
        "hqk,khd->qhd", enc_weights, value_block, preferred_element_type=jnp.float32
    )
    enc_context = enc_context.astype(jnp.bfloat16).reshape(frames_dev, heads_dev * head_size)
    share = frames_dev // head_count
    enc_term = jnp.dot(enc_context, enc_wo, preferred_element_type=jnp.float32)
    mixed = jnp.sum(
        lax.all_to_all(
            enc_term.astype(jnp.bfloat16).reshape(head_count, share, enc_width),
            "heads",
            0,
            0,
            tiled=True,
        ).astype(jnp.float32),
        axis=0,
    )
    own_audio = lax.dynamic_slice_in_dim(audio, head_index * share, share, 0)
    enc_out = (own_audio.astype(jnp.float32) + mixed + enc_bo).astype(jnp.bfloat16)
    groups = dec_wkv.shape[1]
    groups_dev = groups // head_count
    pair_width = dec_wkv.shape[2]
    dec_head = pair_width // 2
    band_bias = jnp.concatenate([jnp.zeros_like(dec_bv), dec_bv], axis=1)
    share_pairs = (
        jnp.dot(
            enc_out,
            dec_wkv.reshape(enc_width, groups * pair_width),
            preferred_element_type=jnp.float32,
        )
        + band_bias.reshape(groups * pair_width)
    ).astype(jnp.bfloat16)
    band_pairs = lax.all_to_all(share_pairs, "heads", 1, 0, tiled=True)
    band_pairs = band_pairs.reshape(frames_dev, groups_dev, pair_width)
    band_wide = with_halo(band_pairs, (("seq", 0),), BAND)
    rows_dev = text.shape[0]
    model_width = text.shape[1]
    query_width = dec_wq.shape[1]
    query_heads = query_width // (groups_dev * dec_head)
    normed = rms_norm(text, norm_gain).astype(jnp.bfloat16)
    query_sum = jnp.dot(
        normed,
        lax.all_gather(dec_wq, "seq", axis=0, tiled=True),
        preferred_element_type=jnp.float32,
    )
    dec_query = (
        (query_sum + dec_bq)
        .astype(jnp.bfloat16)
        .reshape(rows_dev, groups_dev, query_heads, dec_head)
    )
    band_extent = band_wide.shape[0]
    band_keys = band_wide[:, :, :dec_head]
    band_values = band_wide[:, :, dec_head:]
    dec_scores = jnp.einsum(
        "rgqd,kgd->rgqk", dec_query, band_keys, preferred_element_type=jnp.float32
    ) * dec_head ** (-0.5)
    band_frames = seq_index * frames_dev - BAND + jnp.arange(band_extent, dtype=jnp.int32)
    in_band = (band_frames[None, :] >= span_start[:, None]) & (
        band_frames[None, :] < (span_start + span_len)[:, None]
    )
    dec_weights = masked_softmax(dec_scores, in_band[:, None, None, :])
    dec_context = jnp.einsum(
        "rgqk,kgd->rgqd", dec_weights, band_values, preferred_element_type=jnp.float32
    )
    dec_context = dec_context.astype(jnp.bfloat16).reshape(rows_dev, query_width)
    ratio = seq_count // head_count
    set_rows = dec_wo.shape[0]
    block_cols = dec_wo.shape[1]
    flat = [(c, j) for c in range(seq_count) for j in range(head_count)]
    regroup = [
        (c * head_count + j, (ratio * j + c % ratio) * head_count + c // ratio) for c, j in flat
    ]
    piece = lax.ppermute(dec_wo, ("seq", "heads"), regroup)
    pieces, owners = heads_ring_gather(dec_context, "heads")
    set_cols = ratio * block_cols
    column_weight = lax.all_gather(piece, "seq", axis=1, tiled=True)
    total = jnp.zeros((rows_dev, set_cols), jnp.float32)
    for held, owner in zip(pieces, owners):
        for offset in range(held.shape[0]):
            weight_set = lax.dynamic_slice_in_dim(
                column_weight, (owner * held.shape[0] + offset) * set_cols, set_cols, 1
            )
            term = jnp.dot(held[offset], weight_set, preferred_element_type=jnp.float32)
            total = total + term.astype(jnp.bfloat16).astype(jnp.float32)
    summed = total
    col_share = model_width // head_count
    own_text = lax.dynamic_slice_in_dim(text, head_index * col_share, col_share, 1)
    dec_out = (own_text.astype(jnp.float32) + summed).astype(jnp.bfloat16)
    return (enc_out, dec_out)


def solution(mesh):
    return jax.shard_map(
        shards,
        mesh=mesh,
        in_specs=(
            P("seq", None),
            P(),
            P(),
            P(None, "heads"),
            P("heads"),
            P(None, "heads"),
            P(None, "heads"),
            P("heads"),
            P("heads", None),
            P(),
            P("heads"),
            P(),
            P(),
            P("seq", None),
            P(),
            P("seq", "heads"),
            P("heads"),
            P("heads", "seq"),
            P("seq"),
            P("seq"),
        ),
        out_specs=(P(("seq", "heads"), None), P("seq", "heads")),
        check_vma=False,
    )
```

profile of v0, /device:TPU:1, one launch (start us, length us, event | category | flops | bytes accessed | tf_op | source)
XLA Modules:
  0.0 194.4 jit_solution(3535932592329753961)
XLA Ops:
  8.0 6.0 %collective-permute-start.5 = (bf16[512,512]{1,0:T(8,128)(2,1)}, bf16[512,512]{1,0:T(8,128)(2,1)S(1)}, u32[]{:S(2)}, u32[]{:S(2)}) collective-permute-start(bf16[512,512]{1,0:T(8,128)(2,1)} %param.37), channel_id=1, source_target_pairs={{0,0},{1,16},{2,32},{3,48},{4,64},{5,80},{6,96},{7,112},{8,8},{9,2... | collective-permute-start | bytes 1572872 | tf_op jit(solution)/shard_map/ppermute | solution.py:204
  14.0 7.1 %collective-permute-done.5 = bf16[512,512]{1,0:T(8,128)(2,1)S(1)} collective-permute-done((bf16[512,512]{1,0:T(8,128)(2,1)}, bf16[512,512]{1,0:T(8,128)(2,1)S(1)}, u32[]{:S(2)}, u32[]{:S(2)}) %collective-permute-start.5) | collective-permute-done | bytes 524320 | tf_op jit(solution)/shard_map/ppermute | solution.py:204
  23.2 1.5 fusion.25
  24.7 1.4 fusion.28
  28.8 3.1 %collective-permute-start = (bf16[128,2,128]{2,0,1:T(8,128)(2,1)S(1)}, bf16[128,2,128]{2,0,1:T(8,128)(2,1)S(1)}, u32[]{:S(2)}, u32[]{:S(2)}) collective-permute-start(bf16[128,2,128]{2,0,1:T(8,128)(2,1)S(1)} %get-tuple-element.4), channel_id=1, source_target_pairs={{0,8},{8,16},{16,24},{24,32},{32,40},{40,48},{48,56},{56,64},{64,7... | collective-permute-start | bytes 196616 | tf_op jit(solution)/shard_map/ppermute | solution.py:15
  33.9 7.1 %copy.45 = bf16[160,8,8,256]{3,1,2,0:T(8,128)(2,1)} copy(bf16[160,8,8,256]{3,2,1,0:T(8,128)(2,1)} %bitcast.108) | data formatting | bytes 10485760
  45.4 24.3 %all-to-all-start = ((bf16[8,32,1280]{2,1,0:T(8,128)(2,1)}), bf16[8,32,1280]{2,1,0:T(8,128)(2,1)S(1)}, u32[]{:S(2)}, u32[]{:S(2)}) async-start(bf16[8,32,1280]{2,1,0:T(8,128)(2,1)} %bitcast.7), calls=%async_computation | async-start | bytes 1310720 | tf_op jit(solution)/shard_map/all_to_all | solution.py:140
  69.8 5.3 %fusion.1 = f32[512]{0:T(512)S(1)} fusion(bf16[512,8192]{1,0:T(8,128)(2,1)} %param.33), kind=kLoop, calls=%fused_computation.3 | loop fusion | flops 12582400 | bytes 8390656 | tf_op jit(solution)/shard_map/reduce_sum | solution.py:70
  75.1 5.5 %all-to-all-done = bf16[8,32,1280]{2,1,0:T(8,128)(2,1)S(1)} async-done(((bf16[8,32,1280]{2,1,0:T(8,128)(2,1)}), bf16[8,32,1280]{2,1,0:T(8,128)(2,1)S(1)}, u32[]{:S(2)}, u32[]{:S(2)}) %all-to-all-start) | async-done | bytes 655392 | tf_op jit(solution)/shard_map/all_to_all | solution.py:140
  81.6 3.7 %fusion.14 = bf16[32,2048]{1,0:T(8,128)(2,1)S(1)} fusion(bf16[32,1280]{1,0:T(8,128)(2,1)S(1)} %add_convert_fusion.1, bf16[1280,2048]{1,0:T(8,128)(2,1)} %bitcast.107, f32[2048]{0:T(1024)S(1)} %bitcast.121), kind=kOutput, calls=%fused_computation.20 | convolution fusion | flops 167903232 | bytes 5464064 | tf_op jit(solution)/shard_map/dot_general | solution.py:157
  85.9 4.3 %all-to-all-start.1 = ((bf16[32,8,256]{2,0,1:T(8,128)(2,1)}), bf16[32,8,256]{2,0,1:T(8,128)(2,1)S(1)}, u32[]{:S(2)}, u32[]{:S(2)}) async-start(bf16[32,8,256]{2,0,1:T(8,128)(2,1)} %bitcast.106), calls=%async_computation.1 | async-start | bytes 262144 | tf_op jit(solution)/shard_map/all_to_all | solution.py:164
  90.5 4.9 %all-to-all-done.1 = bf16[32,8,256]{2,0,1:T(8,128)(2,1)S(1)} async-done(((bf16[32,8,256]{2,0,1:T(8,128)(2,1)}), bf16[32,8,256]{2,0,1:T(8,128)(2,1)S(1)}, u32[]{:S(2)}, u32[]{:S(2)}) %all-to-all-start.1) | async-done | bytes 131104 | tf_op jit(solution)/shard_map/all_to_all | solution.py:164
  96.7 5.0 %collective-permute-start.2 = (bf16[256,1,256]{2,0,1:T(8,128)(2,1)S(1)}, bf16[256,1,256]{2,0,1:T(8,128)(2,1)S(1)}, u32[]{:S(2)}, u32[]{:S(2)}) collective-permute-start(bf16[256,1,256]{2,0,1:T(8,128)(2,1)S(1)} %bitcast.116), channel_id=1, source_target_pairs={{0,8},{8,16},{16,24},{24,32},{32,40},{40,48},{48,56},{56,64},{64,7... | collective-permute-start | bytes 393224 | tf_op jit(solution)/shard_map/ppermute | solution.py:15
  103.5 10.9 %fusion.35 = bf16[512,512]{0,1:T(8,128)(2,1)S(1)} fusion(bf16[8192,512]{1,0:T(8,128)(2,1)} %all-gather.3.cloned.1.call-done, bf16[512,8192]{1,0:T(8,128)(2,1)} %param.33, f32[8192]{0:T(1024)S(1)} %copy-done.9, f32[512]{0:T(512)S(1)} %add_rsqrt_fusion, f32[512]{0:T(512)S(1)} %copy-done.10), kind=kOutput, calls=%fused_computation.48 | convolution fusion | flops 4312268800 | bytes 17338368 | tf_op jit(solution)/shard_map/dot_general | solution.py:172
  117.0 2.1 %fusion.32 = bf16[128,512,4]{1,0,2:T(8,128)(2,1)S(1)} fusion(f32[512,4]{0,1:T(4,128)S(1)} %fusion.11, f32[512,4]{0,1:T(4,128)S(1)} %get-tuple-element.6, f32[768,512,4]{1,0,2:T(8,128)S(1)} %get-tuple-element.7, pred[512,768]{0,1:T(8,128)(4,1)S(1)} %compare_and_fusion, bf16[768,1,256]{2,0,1:T(8,128)(2,1)S(1)} %pad_maximum_fusion), kind=kOutput, calls=%fused_computation.47 | convolution fusion | flops 410779648 | bytes 7421952 | tf_op jit(solution)/shard_map/rgqk,kgd->rgqd/dot_general | solution.py:193
  119.1 1.9 collective-permute-start.4
  120.9 1.5 collective-permute-done.4
  123.6 13.2 %collective-permute-done.6 = bf16[2,512,512]{1,2,0:T(8,128)(2,1)S(1)} collective-permute-done((bf16[2,512,512]{1,2,0:T(8,128)(2,1)S(1)}, bf16[2,512,512]{1,2,0:T(8,128)(2,1)S(1)}, u32[]{:S(2)}, u32[]{:S(2)}) %collective-permute-start.6) | collective-permute-done | bytes 1048608 | tf_op jit(solution)/shard_map/ppermute | solution.py:53
  136.8 2.1 %collective-permute-start.7 = (bf16[2,512,512]{1,2,0:T(8,128)(2,1)S(1)}, bf16[2,512,512]{1,2,0:T(8,128)(2,1)S(1)}, u32[]{:S(2)}, u32[]{:S(2)}) collective-permute-start(bf16[2,512,512]{1,2,0:T(8,128)(2,1)S(1)} %collective-permute-done.6), channel_id=1, source_target_pairs={{0,2},{1,7},{2,4},{3,1},{4,6},{5,3},{6,0},{7,5},{8,10},{9,15},{10,... | collective-permute-start | bytes 3145736 | tf_op jit(solution)/shard_map/ppermute | solution.py:54
  138.8 34.2 %all-gather.5.cloned.1.call-done = bf16[512,8192]{1,0:T(8,128)(2,1)} async-done(((bf16[512,512]{1,0:T(8,128)(2,1)}), bf16[512,8192]{1,0:T(8,128)(2,1)}) %all-gather.5.cloned.1.call-update) | async-done | bytes 8388624 | tf_op jit(solution)/shard_map/all_gather | solution.py:207
  173.1 2.1 %convolution_convert_fusion.7 = bf16[512,1024]{1,0:T(8,128)(2,1)S(1)} fusion(bf16[512,8192]{1,0:T(8,128)(2,1)} %all-gather.5.cloned.1.call-done, s32[]{:T(128)S(6)} %select_n.88, bf16[2,512,512]{1,2,0:T(8,128)(2,1)S(1)} %maximum_select_fusion), kind=kOutput, calls=%fused_computation.33 | convolution fusion | flops 537395200 | bytes 2621444 | tf_op jit(solution)/shard_map/dot_general | solution.py:214
  175.2 2.5 %convolution_convert_fusion.8 = bf16[512,1024]{1,0:T(8,128)(2,1)S(1)} fusion(bf16[512,8192]{1,0:T(8,128)(2,1)} %all-gather.5.cloned.1.call-done, s32[]{:T(128)S(6)} %select_n.87, bf16[2,512,512]{1,2,0:T(8,128)(2,1)S(1)} %maximum_select_fusion), kind=kOutput, calls=%fused_computation.34 | convolution fusion | flops 537395200 | bytes 2621444 | tf_op jit(solution)/shard_map/dot_general | solution.py:214
  177.7 2.3 %collective-permute-start.8 = (bf16[2,512,512]{1,2,0:T(8,128)(2,1)S(1)}, bf16[2,512,512]{1,2,0:T(8,128)(2,1)S(1)}, u32[]{:S(2)}, u32[]{:S(2)}) collective-permute-start(bf16[2,512,512]{1,2,0:T(8,128)(2,1)S(1)} %collective-permute-done.6), channel_id=1, source_target_pairs={{0,1},{1,0},{2,3},{3,2},{4,5},{5,4},{6,7},{7,6},{8,9},{9,8},{10,11... | collective-permute-start | bytes 3145736 | tf_op jit(solution)/shard_map/ppermute | solution.py:55
  183.8 3.8 %add_convert_fusion = bf16[512,1024]{1,0:T(8,128)(2,1)} fusion(bf16[512,1024]{1,0:T(8,128)(2,1)S(1)} %convolution_convert_fusion.2, bf16[512,1024]{1,0:T(8,128)(2,1)S(1)} %convolution_convert_fusion.3, bf16[512,1024]{1,0:T(8,128)(2,1)S(1)} %convolution_convert_fusion.4, bf16[512,1024]{1,0:T(8,128)(2,1)S(1)} %convolution_convert_fusion.5, ...), kind=kOutput, calls=%fused_computation.21 | convolution fusion | flops 546832384 | bytes 11010056 | tf_op jit(solution)/shard_map/dot_general | solution.py:214
  (75 shorter events, 24.3 us)
Async XLA Ops:
  7.2 37.1 %copy-start = (bf16[128,1280]{1,0:T(8,128)(2,1)S(1)}, bf16[128,1280]{1,0:T(8,128)(2,1)}, u32[]{:S(2)}) copy-start(bf16[128,1280]{1,0:T(8,128)(2,1)} %param.28) | copy-start | bytes 983044
  7.2 96.3 %all-gather.3.cloned.1.call-start = ((), (), s32[]{:S(2)}) async-start(), calls=%async_computation.2 | async-start | bytes 8912896 | tf_op jit(solution)/shard_map/all_gather | solution.py:174
  7.9 165.2 %all-gather.5.cloned.1.call-start = ((), (), s32[]{:S(2)}) async-start(), calls=%async_computation.3 | async-start | bytes 8912896 | tf_op jit(solution)/shard_map/all_gather | solution.py:207
  8.0 13.1 %collective-permute-start.5 = (bf16[512,512]{1,0:T(8,128)(2,1)}, bf16[512,512]{1,0:T(8,128)(2,1)S(1)}, u32[]{:S(2)}, u32[]{:S(2)}) collective-permute-start(bf16[512,512]{1,0:T(8,128)(2,1)} %param.37), channel_id=1, source_target_pairs={{0,0},{1,16},{2,32},{3,48},{4,64},{5,80},{6,96},{7,112},{8,8},{9,2... | collective-permute-start | bytes 1572872 | tf_op jit(solution)/shard_map/ppermute | solution.py:204
  26.1 14.9 %copy-start.4 = (s32[512]{0:T(512)S(1)}, s32[512]{0:T(512)}, u32[]{:S(2)}) copy-start(s32[512]{0:T(512)} %param.38) | copy-start | bytes 6148
  26.1 14.9 %copy-start.6 = (s32[512]{0:T(512)S(1)}, s32[512]{0:T(512)}, u32[]{:S(2)}) copy-start(s32[512]{0:T(512)} %param.39) | copy-start | bytes 6148
  27.4 13.8 %copy-start.2 = (bf16[1280,128]{1,0:T(8,128)(2,1)S(1)}, bf16[1280,128]{1,0:T(8,128)(2,1)}, u32[]{:S(2)}) copy-start(bf16[1280,128]{1,0:T(8,128)(2,1)} %param.23) | copy-start | bytes 983044
  27.4 13.8 %copy-start.7 = (f32[128]{0:T(128)S(1)}, f32[128]{0:T(128)}, u32[]{:S(2)}) copy-start(f32[128]{0:T(128)} %param.24) | copy-start | bytes 1540
  28.8 12.8 %collective-permute-start = (bf16[128,2,128]{2,0,1:T(8,128)(2,1)S(1)}, bf16[128,2,128]{2,0,1:T(8,128)(2,1)S(1)}, u32[]{:S(2)}, u32[]{:S(2)}) collective-permute-start(bf16[128,2,128]{2,0,1:T(8,128)(2,1)S(1)} %get-tuple-element.4), channel_id=1, source_target_pairs={{0,8},{8,16},{16,24},{24,32},{32,40},{40,48},{48,56},{56,64},{64,7... | collective-permute-start | bytes 196616 | tf_op jit(solution)/shard_map/ppermute | solution.py:15
  31.9 9.7 %collective-permute-start.1 = (bf16[128,2,128]{2,0,1:T(8,128)(2,1)S(1)}, bf16[128,2,128]{2,0,1:T(8,128)(2,1)S(1)}, u32[]{:S(2)}, u32[]{:S(2)}) collective-permute-start(bf16[128,2,128]{2,0,1:T(8,128)(2,1)S(1)} %get-tuple-element.5), channel_id=1, source_target_pairs={{8,0},{16,8},{24,16},{32,24},{40,32},{48,40},{56,48},{64,56},{72,6... | collective-permute-start | bytes 196616 | tf_op jit(solution)/shard_map/ppermute | solution.py:18
  33.9 8.4 %copy-start.11 = (s32[2]{0:T(128)S(1)}, s32[2]{0:T(128)}, u32[]{:S(2)}) copy-start(s32[2]{0:T(128)} %param.30) | copy-start | bytes 28
  44.2 36.4 %copy-start.5 = (f32[1280]{0:T(1024)S(1)}, f32[1280]{0:T(1024)}, u32[]{:S(2)}) copy-start(f32[1280]{0:T(1024)} %param.29) | copy-start | bytes 15364
  45.4 35.1 %all-to-all-start = ((bf16[8,32,1280]{2,1,0:T(8,128)(2,1)}), bf16[8,32,1280]{2,1,0:T(8,128)(2,1)S(1)}, u32[]{:S(2)}, u32[]{:S(2)}) async-start(bf16[8,32,1280]{2,1,0:T(8,128)(2,1)} %bitcast.7), calls=%async_computation | async-start | bytes 1310720 | tf_op jit(solution)/shard_map/all_to_all | solution.py:140
  69.8 33.7 %copy-start.9 = (f32[8192]{0:T(1024)S(1)}, f32[8192]{0:T(1024)}, u32[]{:S(2)}) copy-start(f32[8192]{0:T(1024)} %param.34) | copy-start | bytes 98308
  69.8 33.7 %copy-start.10 = (f32[512]{0:T(512)S(1)}, f32[512]{0:T(512)}, u32[]{:S(2)}) copy-start(f32[512]{0:T(512)} %param.36) | copy-start | bytes 6148
  81.6 32.9 %copy-start.3 = (bf16[32,1280]{1,0:T(8,128)(2,1)}, bf16[32,1280]{1,0:T(8,128)(2,1)S(1)}, u32[]{:S(2)}) copy-start(bf16[32,1280]{1,0:T(8,128)(2,1)S(1)} %add_convert_fusion.1) | copy-start | bytes 245764
  85.9 9.5 %all-to-all-start.1 = ((bf16[32,8,256]{2,0,1:T(8,128)(2,1)}), bf16[32,8,256]{2,0,1:T(8,128)(2,1)S(1)}, u32[]{:S(2)}, u32[]{:S(2)}) async-start(bf16[32,8,256]{2,0,1:T(8,128)(2,1)} %bitcast.106), calls=%async_computation.1 | async-start | bytes 262144 | tf_op jit(solution)/shard_map/all_to_all | solution.py:164
  95.4 7.2 %collective-permute-start.3 = (bf16[256,1,256]{2,0,1:T(8,128)(2,1)S(1)}, bf16[256,1,256]{2,0,1:T(8,128)(2,1)S(1)}, u32[]{:S(2)}, u32[]{:S(2)}) collective-permute-start(bf16[256,1,256]{2,0,1:T(8,128)(2,1)S(1)} %bitcast.115), channel_id=1, source_target_pairs={{8,0},{16,8},{24,16},{32,24},{40,32},{48,40},{56,48},{64,56},{72,6... | collective-permute-start | bytes 393224 | tf_op jit(solution)/shard_map/ppermute | solution.py:18
  96.7 6.7 %collective-permute-start.2 = (bf16[256,1,256]{2,0,1:T(8,128)(2,1)S(1)}, bf16[256,1,256]{2,0,1:T(8,128)(2,1)S(1)}, u32[]{:S(2)}, u32[]{:S(2)}) collective-permute-start(bf16[256,1,256]{2,0,1:T(8,128)(2,1)S(1)} %bitcast.116), channel_id=1, source_target_pairs={{0,8},{8,16},{16,24},{24,32},{32,40},{40,48},{48,56},{56,64},{64,7... | collective-permute-start | bytes 393224 | tf_op jit(solution)/shard_map/ppermute | solution.py:15
  119.1 3.4 %collective-permute-start.4 = (bf16[512,512]{0,1:T(8,128)(2,1)S(1)}, bf16[512,512]{0,1:T(8,128)(2,1)S(1)}, u32[]{:S(2)}, u32[]{:S(2)}) collective-permute-start(bf16[512,512]{0,1:T(8,128)(2,1)S(1)} %bitcast.109), channel_id=1, source_target_pairs={{0,1},{1,0},{2,3},{3,2},{4,5},{5,4},{6,7},{7,6},{8,9},{9,8},{10,11... | collective-permute-start | bytes 1572872 | tf_op jit(solution)/shard_map/ppermute | solution.py:47
  122.7 14.1 %collective-permute-start.6 = (bf16[2,512,512]{1,2,0:T(8,128)(2,1)S(1)}, bf16[2,512,512]{1,2,0:T(8,128)(2,1)S(1)}, u32[]{:S(2)}, u32[]{:S(2)}) collective-permute-start(bf16[2,512,512]{1,2,0:T(8,128)(2,1)S(1)} %maximum_select_fusion), channel_id=1, source_target_pairs={{0,2},{1,7},{2,4},{3,1},{4,6},{5,3},{6,0},{7,5},{8,10},{9,15},{10,... | collective-permute-start | bytes 3145736 | tf_op jit(solution)/shard_map/ppermute | solution.py:53
  136.8 44.7 %collective-permute-start.7 = (bf16[2,512,512]{1,2,0:T(8,128)(2,1)S(1)}, bf16[2,512,512]{1,2,0:T(8,128)(2,1)S(1)}, u32[]{:S(2)}, u32[]{:S(2)}) collective-permute-start(bf16[2,512,512]{1,2,0:T(8,128)(2,1)S(1)} %collective-permute-done.6), channel_id=1, source_target_pairs={{0,2},{1,7},{2,4},{3,1},{4,6},{5,3},{6,0},{7,5},{8,10},{9,15},{10,... | collective-permute-start | bytes 3145736 | tf_op jit(solution)/shard_map/ppermute | solution.py:54
  173.1 6.9 %copy-start.8 = (bf16[512,8192]{1,0:T(8,128)(2,1)S(1)}, bf16[512,8192]{1,0:T(8,128)(2,1)}, u32[]{:S(2)}) copy-start(bf16[512,8192]{1,0:T(8,128)(2,1)} %all-gather.5.cloned.1.call-done) | copy-start | bytes 25165828
  177.7 5.4 %collective-permute-start.8 = (bf16[2,512,512]{1,2,0:T(8,128)(2,1)S(1)}, bf16[2,512,512]{1,2,0:T(8,128)(2,1)S(1)}, u32[]{:S(2)}, u32[]{:S(2)}) collective-permute-start(bf16[2,512,512]{1,2,0:T(8,128)(2,1)S(1)} %collective-permute-done.6), channel_id=1, source_target_pairs={{0,1},{1,0},{2,3},{3,2},{4,5},{5,4},{6,7},{7,6},{8,9},{9,8},{10,11... | collective-permute-start | bytes 3145736 | tf_op jit(solution)/shard_map/ppermute | solution.py:55
  (1 other events, 0.8 us)
Sparse Core Ops, SparseCore 0:
  10.1 85.0 all-gather.2
  97.3 75.7 all-gather.4
where the time goes:
time: 195 us; the launch traced here: 194 us
  waiting for transfers between devices  68.8 us (35%)
  starting transfers between devices  52.6 us (27%)
  matrix products  35.7 us (18%)
  between operations  14.5 us (7%)
  other arithmetic  13.3 us (7%)
  local copies, waits for them, and re-layouts  9.56 us (5%)
    all_gather x1, waiting for transfers between devices, shards(): column_weight = lax.all_gather(piece, 'seq', axis=1, tiled=True)  34.2 us
    all_to_all x1, starting transfers between devices, shards(): lax.all_to_all(enc_term.astype(jnp.bfloat16).reshape(head_count, share, e...  24.3 us
    ppermute x1, waiting for transfers between devices, heads_ring_gather(): near = lax.ppermute(own, axis, step)  13.2 us
    dot_general x8, matrix products, shards(): term = jnp.dot(held[offset], weight_set, preferred_element_type=jnp.float32)  12 us
    dot_general x1, matrix products, shards(): jnp.dot(normed, lax.all_gather(dec_wq, 'seq', axis=0, tiled=True), prefer...  10.9 us
    unnamed x27, local copies, waits for them, and re-layouts  8.65 us
    ppermute x2, starting transfers between devices, with_halo(): lax.ppermute(lax.slice_in_dim(block, block.shape[dim] - width, None, axis...  8.07 us
    ppermute x1, waiting for transfers between devices, shards(): piece = lax.ppermute(dec_wo, ('seq', 'heads'), regroup)  7.06 us
  transfers between devices with their start and end apart: 13, of which 8 were waited for; matrix products, arithmetic and copies ran while one was open for 27% of the time, Pallas kernels for 0%

commit v1 on v0

--- a/solution.py
+++ b/solution.py
@@ -204,7 +204,9 @@
     piece = lax.ppermute(dec_wo, ("seq", "heads"), regroup)
     pieces, owners = heads_ring_gather(dec_context, "heads")
     set_cols = ratio * block_cols
-    column_weight = lax.all_gather(piece, "seq", axis=1, tiled=True)
+    column_weight = jnp.concatenate(
+        lax.all_to_all(jnp.stack([piece] * lax.axis_size("seq")), "seq", 0, 0), axis=1
+    )
     total = jnp.zeros((rows_dev, set_cols), jnp.float32)
     for held, owner in zip(pieces, owners):
         for offset in range(held.shape[0]):

time: 195 us -> 287 us (1.47)
  the two profiles are of different devices: /device:TPU:1 before, /device:TPU:118 now
where the time goes in v1:
time: 287 us; the launch traced here: 286 us
  waiting for transfers between devices  165 us (57%)
  matrix products  41.9 us (15%)
  starting transfers between devices  38.8 us (14%)
  between operations  14.6 us (5%)
  other arithmetic  13.1 us (5%)
  local copies, waits for them, and re-layouts  12.4 us (4%)
    ppermute x2, waiting for transfers between devices, with_halo(): lax.ppermute(lax.slice_in_dim(block, 0, width, axis=dim), axis, backward)  100 us
    ppermute x2, waiting for transfers between devices, with_halo(): lax.ppermute(lax.slice_in_dim(block, block.shape[dim] - width, None, axis...  31.6 us
    dot_general x8, matrix products, shards(): term = jnp.dot(held[offset], weight_set, preferred_element_type=jnp.float32)  18 us
    ppermute x1, waiting for transfers between devices, heads_ring_gather(): near = lax.ppermute(own, axis, step)  14.7 us
    all_to_all x1, starting transfers between devices, shards(): lax.all_to_all(jnp.stack([piece] * lax.axis_size('seq')), 'seq', 0, 0)  12.3 us
    dot_general x1, matrix products, shards(): jnp.dot(normed, lax.all_gather(dec_wq, 'seq', axis=0, tiled=True), prefer...  10.4 us
    all_to_all x1, starting transfers between devices, shards(): band_pairs = lax.all_to_all(share_pairs, 'heads', 1, 0, tiled=True)  9.55 us
    unnamed x25, local copies, waits for them, and re-layouts  7.23 us
  transfers between devices with their start and end apart: 13, of which 8 were waited for; matrix products, arithmetic and copies ran while one was open for 21% of the time, Pallas kernels for 0%

profile of v1, /device:TPU:118, one launch (start us, length us, event | category | flops | bytes accessed | tf_op | source)
XLA Modules:
  0.0 285.7 jit_solution(16833960740459727969)
XLA Ops:
  14.6 2.7 collective-permute-start.1
  20.3 3.7 %collective-permute-done = bf16[128,2,128]{2,0,1:T(8,128)(2,1)S(1)} collective-permute-done((bf16[128,2,128]{2,0,1:T(8,128)(2,1)S(1)}, bf16[128,2,128]{2,0,1:T(8,128)(2,1)S(1)}, u32[]{:S(2)}, u32[]{:S(2)}) %collective-permute-start) | collective-permute-done | bytes 65568 | tf_op jit(solution)/shard_map/ppermute | solution.py:15
  27.7 4.9 %all-to-all-start = ((bf16[8,32,1280]{2,1,0:T(8,128)(2,1)}), bf16[8,32,1280]{2,1,0:T(8,128)(2,1)S(1)}, u32[]{:S(2)}, u32[]{:S(2)}) async-start(bf16[8,32,1280]{2,1,0:T(8,128)(2,1)} %bitcast.7), calls=%async_computation | async-start | bytes 1310720 | tf_op jit(solution)/shard_map/all_to_all | solution.py:140
  32.6 3.2 %collective-permute-start.5 = (bf16[512,512]{1,0:T(8,128)(2,1)S(1)}, bf16[512,512]{1,0:T(8,128)(2,1)S(1)}, u32[]{:S(2)}, u32[]{:S(2)}) collective-permute-start(bf16[512,512]{1,0:T(8,128)(2,1)S(1)} %copy-done.7), channel_id=1, source_target_pairs={{0,0},{1,16},{2,32},{3,48},{4,64},{5,80},{6,96},{7,112},{8,8},{9,2... | collective-permute-start | bytes 1572872 | tf_op jit(solution)/shard_map/ppermute | solution.py:204
  35.9 7.2 %copy.47 = bf16[160,8,8,256]{3,1,2,0:T(8,128)(2,1)} copy(bf16[160,8,8,256]{3,2,1,0:T(8,128)(2,1)} %bitcast.111) | data formatting | bytes 10485760
  43.0 6.2 %all-to-all-done = bf16[8,32,1280]{2,1,0:T(8,128)(2,1)S(1)} async-done(((bf16[8,32,1280]{2,1,0:T(8,128)(2,1)}), bf16[8,32,1280]{2,1,0:T(8,128)(2,1)S(1)}, u32[]{:S(2)}, u32[]{:S(2)}) %all-to-all-start) | async-done | bytes 655392 | tf_op jit(solution)/shard_map/all_to_all | solution.py:140
  50.3 3.5 %fusion.14 = bf16[32,2048]{1,0:T(8,128)(2,1)S(1)} fusion(bf16[32,1280]{1,0:T(8,128)(2,1)S(1)} %add_convert_fusion.1, bf16[1280,2048]{1,0:T(8,128)(2,1)} %bitcast.110, f32[2048]{0:T(1024)S(1)} %bitcast.124), kind=kOutput, calls=%fused_computation.20 | convolution fusion | flops 167903232 | bytes 5464064 | tf_op jit(solution)/shard_map/dot_general | solution.py:157
  54.5 9.6 %all-to-all-start.1 = ((bf16[32,8,256]{2,0,1:T(8,128)(2,1)}), bf16[32,8,256]{2,0,1:T(8,128)(2,1)S(1)}, u32[]{:S(2)}, u32[]{:S(2)}) async-start(bf16[32,8,256]{2,0,1:T(8,128)(2,1)} %bitcast.109), calls=%async_computation.1 | async-start | bytes 262144 | tf_op jit(solution)/shard_map/all_to_all | solution.py:164
  64.3 3.2 %all-to-all-done.1 = bf16[32,8,256]{2,0,1:T(8,128)(2,1)S(1)} async-done(((bf16[32,8,256]{2,0,1:T(8,128)(2,1)}), bf16[32,8,256]{2,0,1:T(8,128)(2,1)S(1)}, u32[]{:S(2)}, u32[]{:S(2)}) %all-to-all-start.1) | async-done | bytes 131104 | tf_op jit(solution)/shard_map/all_to_all | solution.py:164
  67.4 4.0 %stack.20 = bf16[16,512,512]{1,2,0:T(8,128)(2,1)} broadcast(bf16[512,512]{0,1:T(8,128)(2,1)S(1)} %copy.41), dimensions={1,2} | broadcast | bytes 8912896 | tf_op jit(solution)/shard_map/stack | solution.py:208
  71.5 12.3 %all-to-all-start.2 = ((bf16[16,512,512]{1,2,0:T(8,128)(2,1)}), bf16[16,512,512]{1,2,0:T(8,128)(2,1)}, u32[]{:S(2)}, u32[]{:S(2)}) async-start(bf16[16,512,512]{1,2,0:T(8,128)(2,1)} %stack.20), calls=%async_computation.2 | async-start | bytes 16777216 | tf_op jit(solution)/shard_map/all_to_all | solution.py:208
  84.2 5.2 %fusion.1 = f32[512]{0:T(512)S(1)} fusion(bf16[512,8192]{1,0:T(8,128)(2,1)} %param.33), kind=kLoop, calls=%fused_computation.3 | loop fusion | flops 12582400 | bytes 8390656 | tf_op jit(solution)/shard_map/reduce_sum | solution.py:70
  89.5 2.8 collective-permute-start.3
  93.8 100.2 %collective-permute-done.3 = bf16[256,1,256]{2,0,1:T(8,128)(2,1)S(1)} collective-permute-done((bf16[256,1,256]{2,0,1:T(8,128)(2,1)S(1)}, bf16[256,1,256]{2,0,1:T(8,128)(2,1)S(1)}, u32[]{:S(2)}, u32[]{:S(2)}) %collective-permute-start.3) | collective-permute-done | bytes 131104 | tf_op jit(solution)/shard_map/ppermute | solution.py:18
  193.9 27.9 %collective-permute-done.2 = bf16[256,1,256]{2,0,1:T(8,128)(2,1)S(1)} collective-permute-done((bf16[256,1,256]{2,0,1:T(8,128)(2,1)S(1)}, bf16[256,1,256]{2,0,1:T(8,128)(2,1)S(1)}, u32[]{:S(2)}, u32[]{:S(2)}) %collective-permute-start.2) | collective-permute-done | bytes 131104 | tf_op jit(solution)/shard_map/ppermute | solution.py:15
  221.9 10.4 %fusion.35 = bf16[512,512]{0,1:T(8,128)(2,1)S(1)} fusion(bf16[8192,512]{1,0:T(8,128)(2,1)} %all-gather.2.cloned.1.call-done, bf16[512,8192]{1,0:T(8,128)(2,1)} %param.33, f32[8192]{0:T(1024)S(1)} %copy-done.8, f32[512]{0:T(512)S(1)} %add_rsqrt_fusion, f32[512]{0:T(512)S(1)} %copy-done.9), kind=kOutput, calls=%fused_computation.48 | convolution fusion | flops 4312268800 | bytes 17338368 | tf_op jit(solution)/shard_map/dot_general | solution.py:172
  234.8 2.1 fusion.32
  239.3 14.7 %collective-permute-done.6 = bf16[2,512,512]{1,2,0:T(8,128)(2,1)S(1)} collective-permute-done((bf16[2,512,512]{1,2,0:T(8,128)(2,1)S(1)}, bf16[2,512,512]{1,2,0:T(8,128)(2,1)S(1)}, u32[]{:S(2)}, u32[]{:S(2)}) %collective-permute-start.6) | collective-permute-done | bytes 1048608 | tf_op jit(solution)/shard_map/ppermute | solution.py:53
  258.3 2.0 convolution_convert_fusion.5
  260.3 2.0 convolution_convert_fusion.6
  262.3 6.5 %collective-permute-done.7 = bf16[2,512,512]{1,2,0:T(8,128)(2,1)S(1)} collective-permute-done((bf16[2,512,512]{1,2,0:T(8,128)(2,1)S(1)}, bf16[2,512,512]{1,2,0:T(8,128)(2,1)S(1)}, u32[]{:S(2)}, u32[]{:S(2)}) %collective-permute-start.7) | collective-permute-done | bytes 1048608 | tf_op jit(solution)/shard_map/ppermute | solution.py:54
  270.8 2.0 convolution_convert_fusion.4
  272.8 2.0 convolution_convert_fusion.2
  274.8 4.1 %add_convert_fusion = bf16[512,1024]{1,0:T(8,128)(2,1)} fusion(bf16[512,1024]{1,0:T(8,128)(2,1)S(1)} %convolution_convert_fusion.2, bf16[512,1024]{1,0:T(8,128)(2,1)S(1)} %convolution_convert_fusion.3, bf16[512,1024]{1,0:T(8,128)(2,1)S(1)} %convolution_convert_fusion.4, bf16[512,1024]{1,0:T(8,128)(2,1)S(1)} %convolution_convert_fusion.5, ...), kind=kOutput, calls=%fused_computation.21 | convolution fusion | flops 546832384 | bytes 11010056 | tf_op jit(solution)/shard_map/dot_general | solution.py:216
  (74 shorter events, 28.7 us)
Async XLA Ops:
  7.2 19.3 %copy-start = (bf16[128,1280]{1,0:T(8,128)(2,1)S(1)}, bf16[128,1280]{1,0:T(8,128)(2,1)}, u32[]{:S(2)}) copy-start(bf16[128,1280]{1,0:T(8,128)(2,1)} %param.28) | copy-start | bytes 983044
  7.2 17.5 %copy-start.10 = (s32[2]{0:T(128)S(1)}, s32[2]{0:T(128)}, u32[]{:S(2)}) copy-start(s32[2]{0:T(128)} %param.30) | copy-start | bytes 28
  7.2 214.7 %all-gather.2.cloned.1.call-start = ((), (), s32[]{:S(2)}) async-start(), calls=%async_computation.3 | async-start | bytes 8912896 | tf_op jit(solution)/shard_map/all_gather | solution.py:174
  14.6 5.6 %collective-permute-start.1 = (bf16[128,2,128]{2,0,1:T(8,128)(2,1)S(1)}, bf16[128,2,128]{2,0,1:T(8,128)(2,1)S(1)}, u32[]{:S(2)}, u32[]{:S(2)}) collective-permute-start(bf16[128,2,128]{2,0,1:T(8,128)(2,1)S(1)} %get-tuple-element.5), channel_id=1, source_target_pairs={{8,0},{16,8},{24,16},{32,24},{40,32},{48,40},{56,48},{64,56},{72,6... | collective-permute-start | bytes 196616 | tf_op jit(solution)/shard_map/ppermute | solution.py:18
  17.4 6.6 %collective-permute-start = (bf16[128,2,128]{2,0,1:T(8,128)(2,1)S(1)}, bf16[128,2,128]{2,0,1:T(8,128)(2,1)S(1)}, u32[]{:S(2)}, u32[]{:S(2)}) collective-permute-start(bf16[128,2,128]{2,0,1:T(8,128)(2,1)S(1)} %get-tuple-element.4), channel_id=1, source_target_pairs={{0,8},{8,16},{16,24},{24,32},{32,40},{40,48},{48,56},{56,64},{64,7... | collective-permute-start | bytes 196616 | tf_op jit(solution)/shard_map/ppermute | solution.py:15
  24.0 8.6 %copy-start.7 = (bf16[512,512]{1,0:T(8,128)(2,1)S(1)}, bf16[512,512]{1,0:T(8,128)(2,1)}, u32[]{:S(2)}) copy-start(bf16[512,512]{1,0:T(8,128)(2,1)} %param.37) | copy-start | bytes 1572868
  26.5 16.5 %copy-start.5 = (f32[8,128]{1,0:T(8,128)S(1)}, f32[8,128]{1,0:T(8,128)}, u32[]{:S(2)}) copy-start(f32[8,128]{1,0:T(8,128)} %param.32) | copy-start | bytes 12292
  27.7 21.7 %copy-start.4 = (f32[1280]{0:T(1024)S(1)}, f32[1280]{0:T(1024)}, u32[]{:S(2)}) copy-start(f32[1280]{0:T(1024)} %param.29) | copy-start | bytes 15364
  27.7 21.6 %all-to-all-start = ((bf16[8,32,1280]{2,1,0:T(8,128)(2,1)}), bf16[8,32,1280]{2,1,0:T(8,128)(2,1)S(1)}, u32[]{:S(2)}, u32[]{:S(2)}) async-start(bf16[8,32,1280]{2,1,0:T(8,128)(2,1)} %bitcast.7), calls=%async_computation | async-start | bytes 1310720 | tf_op jit(solution)/shard_map/all_to_all | solution.py:140
  32.6 31.4 %collective-permute-start.5 = (bf16[512,512]{1,0:T(8,128)(2,1)S(1)}, bf16[512,512]{1,0:T(8,128)(2,1)S(1)}, u32[]{:S(2)}, u32[]{:S(2)}) collective-permute-start(bf16[512,512]{1,0:T(8,128)(2,1)S(1)} %copy-done.7), channel_id=1, source_target_pairs={{0,0},{1,16},{2,32},{3,48},{4,64},{5,80},{6,96},{7,112},{8,8},{9,2... | collective-permute-start | bytes 1572872 | tf_op jit(solution)/shard_map/ppermute | solution.py:204
  50.3 21.2 %copy-start.2 = (bf16[32,1280]{1,0:T(8,128)(2,1)}, bf16[32,1280]{1,0:T(8,128)(2,1)S(1)}, u32[]{:S(2)}) copy-start(bf16[32,1280]{1,0:T(8,128)(2,1)S(1)} %add_convert_fusion.1) | copy-start | bytes 245764
  54.5 12.9 %all-to-all-start.1 = ((bf16[32,8,256]{2,0,1:T(8,128)(2,1)}), bf16[32,8,256]{2,0,1:T(8,128)(2,1)S(1)}, u32[]{:S(2)}, u32[]{:S(2)}) async-start(bf16[32,8,256]{2,0,1:T(8,128)(2,1)} %bitcast.109), calls=%async_computation.1 | async-start | bytes 262144 | tf_op jit(solution)/shard_map/all_to_all | solution.py:164
  71.5 12.3 %copy-start.3 = (s32[512]{0:T(512)S(1)}, s32[512]{0:T(512)}, u32[]{:S(2)}) copy-start(s32[512]{0:T(512)} %param.38) | copy-start | bytes 6148
  71.5 12.3 %copy-start.6 = (s32[512]{0:T(512)S(1)}, s32[512]{0:T(512)}, u32[]{:S(2)}) copy-start(s32[512]{0:T(512)} %param.39) | copy-start | bytes 6148
  71.5 182.5 %all-to-all-start.2 = ((bf16[16,512,512]{1,2,0:T(8,128)(2,1)}), bf16[16,512,512]{1,2,0:T(8,128)(2,1)}, u32[]{:S(2)}, u32[]{:S(2)}) async-start(bf16[16,512,512]{1,2,0:T(8,128)(2,1)} %stack.20), calls=%async_computation.2 | async-start | bytes 16777216 | tf_op jit(solution)/shard_map/all_to_all | solution.py:208
  83.8 138.1 %copy-start.8 = (f32[8192]{0:T(1024)S(1)}, f32[8192]{0:T(1024)}, u32[]{:S(2)}) copy-start(f32[8192]{0:T(1024)} %param.34) | copy-start | bytes 98308
  83.8 138.1 %copy-start.9 = (f32[512]{0:T(512)S(1)}, f32[512]{0:T(512)}, u32[]{:S(2)}) copy-start(f32[512]{0:T(512)} %param.36) | copy-start | bytes 6148
  89.5 104.5 %collective-permute-start.3 = (bf16[256,1,256]{2,0,1:T(8,128)(2,1)S(1)}, bf16[256,1,256]{2,0,1:T(8,128)(2,1)S(1)}, u32[]{:S(2)}, u32[]{:S(2)}) collective-permute-start(bf16[256,1,256]{2,0,1:T(8,128)(2,1)S(1)} %bitcast.118), channel_id=1, source_target_pairs={{8,0},{16,8},{24,16},{32,24},{40,32},{48,40},{56,48},{64,56},{72,6... | collective-permute-start | bytes 393224 | tf_op jit(solution)/shard_map/ppermute | solution.py:18
  92.3 129.6 %collective-permute-start.2 = (bf16[256,1,256]{2,0,1:T(8,128)(2,1)S(1)}, bf16[256,1,256]{2,0,1:T(8,128)(2,1)S(1)}, u32[]{:S(2)}, u32[]{:S(2)}) collective-permute-start(bf16[256,1,256]{2,0,1:T(8,128)(2,1)S(1)} %bitcast.119), channel_id=1, source_target_pairs={{0,8},{8,16},{16,24},{24,32},{32,40},{40,48},{48,56},{56,64},{64,7... | collective-permute-start | bytes 393224 | tf_op jit(solution)/shard_map/ppermute | solution.py:15
  236.9 2.0 collective-permute-start.4
  239.1 14.9 %collective-permute-start.6 = (bf16[2,512,512]{1,2,0:T(8,128)(2,1)S(1)}, bf16[2,512,512]{1,2,0:T(8,128)(2,1)S(1)}, u32[]{:S(2)}, u32[]{:S(2)}) collective-permute-start(bf16[2,512,512]{1,2,0:T(8,128)(2,1)S(1)} %maximum_select_fusion), channel_id=1, source_target_pairs={{0,2},{1,7},{2,4},{3,1},{4,6},{5,3},{6,0},{7,5},{8,10},{9,15},{10,... | collective-permute-start | bytes 3145736 | tf_op jit(solution)/shard_map/ppermute | solution.py:53
  254.0 14.8 %collective-permute-start.7 = (bf16[2,512,512]{1,2,0:T(8,128)(2,1)S(1)}, bf16[2,512,512]{1,2,0:T(8,128)(2,1)S(1)}, u32[]{:S(2)}, u32[]{:S(2)}) collective-permute-start(bf16[2,512,512]{1,2,0:T(8,128)(2,1)S(1)} %collective-permute-done.6), channel_id=1, source_target_pairs={{0,2},{1,7},{2,4},{3,1},{4,6},{5,3},{6,0},{7,5},{8,10},{9,15},{10,... | collective-permute-start | bytes 3145736 | tf_op jit(solution)/shard_map/ppermute | solution.py:54
  258.0 14.8 %collective-permute-start.8 = (bf16[2,512,512]{1,2,0:T(8,128)(2,1)S(1)}, bf16[2,512,512]{1,2,0:T(8,128)(2,1)S(1)}, u32[]{:S(2)}, u32[]{:S(2)}) collective-permute-start(bf16[2,512,512]{1,2,0:T(8,128)(2,1)S(1)} %collective-permute-done.6), channel_id=1, source_target_pairs={{0,1},{1,0},{2,3},{3,2},{4,5},{5,4},{6,7},{7,6},{8,9},{9,8},{10,11... | collective-permute-start | bytes 3145736 | tf_op jit(solution)/shard_map/ppermute | solution.py:55
  270.8 8.1 %copy-start.1 = (bf16[128,1280]{1,0:T(8,128)(2,1)S(1)}, bf16[128,1280]{1,0:T(8,128)(2,1)}, u32[]{:S(2)}) copy-start(bf16[128,1280]{1,0:T(8,128)(2,1)} %param.28) | copy-start | bytes 983044
Sparse Core Ops, SparseCore 0:
  10.1 170.0 all-gather.1
